TPU v7x, 256 devices: a whole 4x4x8 slice. The times are simulated.
256 devices in a mesh: dp: 4 (over y), seq: 16 (over z, core), tensor: 4 (over x).
Axes of the slice: x: 4, y: 4, z: 8, core: 2. Of those that a mesh axis runs over, the one named last changes fastest.
Arguments:
- queries: bfloat16 [16384, 8192], P(('dp', 'seq'), 'tensor'), parts along dimension 0, may hold values from -110 to 110
- keys_values: bfloat16 [16384, 2, 1024], P(('dp', 'seq'), None, 'tensor'), parts along dimension 0, may hold values from -4.5 to 4.5
- out_weight: bfloat16 [8192, 8192], P('tensor', 'seq'), may hold values from -0.1875 to 0.1875
- residual: bfloat16 [16384, 8192], P(('dp', 'tensor'), 'seq'), parts along dimension 0, may hold values from -3 to 3
- segments: int32 [16384], P('dp'), parts along dimension 0, may hold values from 0 to 3, never falling along the last dimension, each value on 1 to 2048 neighbouring positions
Outputs:
- layer_out: bfloat16 [16384, 8192], P(('dp', 'tensor'), 'seq'), parts along dimension 0
There are 4 independent parts, one for each index of `dp`. A program takes and returns all parts, laid end to end along the dimension named above; an argument that names none is the same for every part. Nothing has to cross between parts.
Inputs may be any that keep to these rules, and one draw needn't show every extreme that they name: `segments`: segment numbers never fall along the tokens.
All inputs are finite; a program needn't handle non-finite values.
Results may differ from a plain program's by a relative error of at most 0.0085.
Values may be sent and summed in bfloat16 or wider, within the bound.
No kernel may reach another device: no remote copies, remote signals or barrier semaphores. Data moves between devices by JAX's collectives and lax.ppermute only.
A program may use at most 128 MiB of HBM per device.

v0:
```python
import jax
import jax.numpy as jnp
import numpy as np
from jax import lax
from jax.sharding import PartitionSpec as P

H = 64
KVH = 8
HD = 128
L = 4096
CHUNKS = 4


def attend_rows(query_head, key_head, value_head, doc_ids, first_row, rows):
    key_end = first_row + rows
    query_block = query_head[first_row:key_end]
    raw_scores = jnp.einsum(
        "qd,kd->qk", query_block, key_head[:key_end], preferred_element_type=jnp.float32
    ) * HD ** (-0.5)
    query_pos = first_row + jnp.arange(rows)[:, None]
    key_pos = jnp.arange(key_end)[None, :]
    same_doc = doc_ids[first_row:key_end, None] == doc_ids[None, :key_end]
    allowed = (key_pos <= query_pos) & same_doc
    masked = jnp.where(allowed, raw_scores, -1e30)
    highest = jnp.max(masked, axis=-1, keepdims=True)
    exponents = jnp.where(allowed, jnp.exp(masked - highest), 0.0)
    weights = (exponents / jnp.sum(exponents, axis=-1, keepdims=True)).astype(jnp.bfloat16)
    blended = jnp.einsum(
        "qk,kd->qd", weights, value_head[:key_end], preferred_element_type=jnp.float32
    )
    return blended.astype(jnp.bfloat16)


def on_device(queries, keys_values, out_weight, residual, segments):
    n_seq = lax.axis_size("seq")
    n_ten = lax.axis_size("tensor")
    seq_idx = lax.axis_index("seq")
    tok_dev = queries.shape[0]
    heads_ten = queries.shape[1] // HD
    heads_dev = heads_ten // n_seq
    assert heads_dev == 1
    group_size = H // KVH
    query_slab = queries.reshape(tok_dev, 1, heads_ten * HD)
    query_all = lax.all_to_all(query_slab, "seq", split_axis=2, concat_axis=0, tiled=True)
    query_head = query_all.reshape(query_all.shape[0], HD)
    rows_all = query_head.shape[0]
    assert rows_all == L
    pair_all = lax.all_gather(keys_values, "seq", axis=0, tiled=True)
    kv_local = seq_idx // group_size
    pair_head = lax.dynamic_slice_in_dim(pair_all, kv_local * HD, HD, axis=2)
    key_head = pair_head[:, 0, :]
    value_head = pair_head[:, 1, :]
    doc_ids = segments
    out_rows = rows_all // n_ten
    block_rows = out_rows // CHUNKS
    pieces = []
    for chunk in range(CHUNKS):
        blocks = [
            attend_rows(
                query_head,
                key_head,
                value_head,
                doc_ids,
                part * out_rows + chunk * block_rows,
                block_rows,
            )
            for part in range(n_ten)
        ]
        chunk_heads = jnp.concatenate(blocks, axis=0)
        gathered = lax.all_gather(chunk_heads, "seq", axis=1, tiled=True)
        projected = jnp.dot(gathered, out_weight, preferred_element_type=jnp.float32)
        pieces.append(lax.psum_scatter(projected, "tensor", scatter_dimension=0, tiled=True))
    summed = jnp.concatenate(pieces, axis=0)
    return (residual.astype(jnp.float32) + summed).astype(jnp.bfloat16)


def solution(mesh):
    placed = (
        P(("dp", "seq"), "tensor"),
        P(("dp", "seq"), None, "tensor"),
        P("tensor", "seq"),
        P(("dp", "tensor"), "seq"),
        P("dp"),
    )
    return jax.shard_map(
        on_device, mesh=mesh, in_specs=placed, out_specs=P(("dp", "tensor"), "seq"), check_vma=False
    )
```

profile of v0, /device:TPU:1, one launch (start us, length us, event | category | flops | bytes accessed | tf_op | source)
XLA Modules:
  0.0 436.0 jit_solution(1249033622516324133)
XLA Ops:
  6.5 1.8 copy.43
  8.4 5.9 %copy.44 = bf16[256,1,2048]{0,1,2:T(2,128)(2,1)} copy(bf16[256,1,2048]{2,0,1:T(8,128)(2,1)} %bitcast.316) | data formatting | bytes 2097152 | tf_op jit(solution)/shard_map/reshape | solution.py:43
  14.8 11.6 %reduce = bf16[2048,256]{1,0:T(8,128)(2,1)S(1)} reduce(bf16[2048,1,256]{2,1,0:T(2,128)(2,1)} %bitcast.306, bf16[]{:T(256)} %broadcast.172), dimensions={1}, to_apply=%bitcast.228.reduce_sub_computation | reduce | bytes 2097154
  26.5 1.1 reshape.191
  27.6 10.0 %all-to-all-start = ((bf16[16,2,16384]{2,1,0:T(2,128)(2,1)}), bf16[16,2,16384]{2,1,0:T(2,128)(2,1)S(1)}, u32[]{:S(2)}, u32[]{:S(2)}) async-start(bf16[16,2,16384]{2,1,0:T(2,128)(2,1)} %reshape.191), calls=%async_computation | async-start | bytes 2097152 | tf_op jit(solution)/shard_map/all_to_all | solution.py:44
  38.3 34.3 %all-to-all-done = bf16[16,2,16384]{2,1,0:T(2,128)(2,1)S(1)} async-done(((bf16[16,2,16384]{2,1,0:T(2,128)(2,1)}), bf16[16,2,16384]{2,1,0:T(2,128)(2,1)S(1)}, u32[]{:S(2)}, u32[]{:S(2)}) %all-to-all-start) | async-done | bytes 1048608 | tf_op jit(solution)/shard_map/all_to_all | solution.py:44
  72.5 3.5 reshape.192
  76.0 1.8 copy.61
  77.8 3.2 fusion.130
  81.0 1.9 fusion.30
  84.0 1.4 fusion.39
  87.6 2.3 fusion.65
  89.8 1.7 fusion.69
  91.6 1.1 convolution_convert_fusion.1
  94.3 1.3 fusion.137
  95.9 1.6 convolution_convert_fusion.4
  100.3 1.3 fusion.41
  101.6 1.1 fusion.134
  102.7 1.8 fusion.32
  104.5 1.0 convolution_convert_fusion.3
  105.5 1.6 fusion.68
  107.1 2.2 fusion.64
  110.4 1.3 fusion.141
  111.9 1.5 fusion.140
  115.2 1.2 fusion.45
  116.4 1.0 fusion.138
  118.3 1.8 fusion.33
  120.1 1.4 fusion.67
  121.4 2.0 fusion.63
  124.6 1.2 fusion.145
  125.9 1.4 fusion.144
  128.8 1.1 fusion.48
  131.6 1.6 fusion.35
  133.3 1.3 fusion.66
  134.6 1.9 fusion.70
  137.3 4.7 %all-gather.14.cloned.1.call-done = bf16[1024,2048]{1,0:T(8,128)(2,1)} async-done(((bf16[1024,128]{1,0:T(8,128)(2,1)}), bf16[1024,2048]{1,0:T(8,128)(2,1)}) %all-gather.14.cloned.1.call-update) | async-done | bytes 4194320 | tf_op jit(solution)/shard_map/all_gather | solution.py:70
  142.0 5.9 %fusion.149 = f32[1024,512]{1,0:T(8,128)} fusion(bf16[1024,2048]{1,0:T(8,128)(2,1)} %all-gather.14.cloned.1.call-done, bf16[2048,512]{1,0:T(8,128)(2,1)S(1)} %copy-done), kind=kOutput, calls=%fused_computation.289 | convolution fusion | flops 2147483648 | bytes 8388608 | tf_op jit(solution)/shard_map/dot_general | solution.py:71
  147.9 43.5 %all-gather.12.cloned.1.call-done = bf16[1024,2048]{1,0:T(8,128)(2,1)} async-done(((bf16[1024,128]{1,0:T(8,128)(2,1)}), bf16[1024,2048]{1,0:T(8,128)(2,1)}) %all-gather.12.cloned.1.call-update) | async-done | bytes 4194320 | tf_op jit(solution)/shard_map/all_gather | solution.py:70
  191.5 5.9 %fusion.148 = f32[1024,512]{1,0:T(8,128)} fusion(bf16[1024,2048]{1,0:T(8,128)(2,1)} %all-gather.12.cloned.1.call-done, bf16[2048,512]{1,0:T(8,128)(2,1)S(1)} %copy-done), kind=kOutput, calls=%fused_computation.288 | convolution fusion | flops 2147483648 | bytes 8388608 | tf_op jit(solution)/shard_map/dot_general | solution.py:71
  197.7 43.0 %all-gather.10.cloned.1.call-done = bf16[1024,2048]{1,0:T(8,128)(2,1)} async-done(((bf16[1024,128]{1,0:T(8,128)(2,1)}), bf16[1024,2048]{1,0:T(8,128)(2,1)}) %all-gather.10.cloned.1.call-update) | async-done | bytes 4194320 | tf_op jit(solution)/shard_map/all_gather | solution.py:70
  240.7 5.8 %fusion.147 = f32[1024,512]{1,0:T(8,128)} fusion(bf16[1024,2048]{1,0:T(8,128)(2,1)} %all-gather.10.cloned.1.call-done, bf16[2048,512]{1,0:T(8,128)(2,1)S(1)} %copy-done), kind=kOutput, calls=%fused_computation.287 | convolution fusion | flops 2147483648 | bytes 8388608 | tf_op jit(solution)/shard_map/dot_general | solution.py:71
  246.6 43.3 %all-gather.8.cloned.1.call-done = bf16[1024,2048]{1,0:T(8,128)(2,1)} async-done(((bf16[1024,128]{1,0:T(8,128)(2,1)}), bf16[1024,2048]{1,0:T(8,128)(2,1)}) %all-gather.8.cloned.1.call-update) | async-done | bytes 4194320 | tf_op jit(solution)/shard_map/all_gather | solution.py:70
  289.9 5.8 %fusion.146 = f32[1024,512]{1,0:T(8,128)} fusion(bf16[1024,2048]{1,0:T(8,128)(2,1)} %all-gather.8.cloned.1.call-done, bf16[2048,512]{1,0:T(8,128)(2,1)S(1)} %copy-done), kind=kOutput, calls=%fused_computation.286 | convolution fusion | flops 2147483648 | bytes 8388608 | tf_op jit(solution)/shard_map/dot_general | solution.py:71
  295.8 26.6 %reduce-scatter.11.cloned.1.call-done = f32[256,512]{1,0:T(8,128)} async-done(((f32[1024,512]{1,0:T(8,128)}), f32[256,512]{1,0:T(8,128)}) %reduce-scatter.11.cloned.1.call-update) | async-done | bytes 524304 | tf_op jit(solution)/shard_map/reduce_scatter | solution.py:72
  322.4 34.6 %reduce-scatter.9.cloned.1.call-done = f32[256,512]{1,0:T(8,128)} async-done(((f32[1024,512]{1,0:T(8,128)}), f32[256,512]{1,0:T(8,128)}) %reduce-scatter.9.cloned.1.call-update) | async-done | bytes 524304 | tf_op jit(solution)/shard_map/reduce_scatter | solution.py:72
  357.0 34.6 %reduce-scatter.7.cloned.1.call-done = f32[256,512]{1,0:T(8,128)} async-done(((f32[1024,512]{1,0:T(8,128)}), f32[256,512]{1,0:T(8,128)}) %reduce-scatter.7.cloned.1.call-update) | async-done | bytes 524304 | tf_op jit(solution)/shard_map/reduce_scatter | solution.py:72
  391.6 34.6 %reduce-scatter.5.cloned.1.call-done = f32[256,512]{1,0:T(8,128)} async-done(((f32[1024,512]{1,0:T(8,128)}), f32[256,512]{1,0:T(8,128)}) %reduce-scatter.5.cloned.1.call-update) | async-done | bytes 524304 | tf_op jit(solution)/shard_map/reduce_scatter | solution.py:72
  426.2 2.8 fusion.36
  (85 shorter events, 18.4 us)
Async XLA Ops:
  6.5 135.5 %copy-start = (bf16[2048,512]{1,0:T(8,128)(2,1)S(1)}, bf16[2048,512]{1,0:T(8,128)(2,1)}, u32[]{:S(2)}) copy-start(bf16[2048,512]{1,0:T(8,128)(2,1)} %param.7) | copy-start | bytes 6291460
  6.5 71.3 %all-gather.6.cloned.1.call-start = ((), (), s32[]{:S(2)}) async-start(), calls=%async_computation.5 | async-start | bytes 4456448 | tf_op jit(solution)/shard_map/all_gather | solution.py:48
  26.5 11.7 %copy-start.1 = (s32[4096]{0:T(1024)S(1)}, s32[4096]{0:T(1024)}, u32[]{:S(2)}) copy-start(s32[4096]{0:T(1024)} %param.9) | copy-start | bytes 49156
  27.6 44.9 %all-to-all-start = ((bf16[16,2,16384]{2,1,0:T(2,128)(2,1)}), bf16[16,2,16384]{2,1,0:T(2,128)(2,1)S(1)}, u32[]{:S(2)}, u32[]{:S(2)}) async-start(bf16[16,2,16384]{2,1,0:T(2,128)(2,1)} %reshape.191), calls=%async_computation | async-start | bytes 2097152 | tf_op jit(solution)/shard_map/all_to_all | solution.py:44
  37.6 104.4 %all-gather.14.cloned.1.call-start = ((), (), s32[]{:S(2)}) async-start(), calls=%async_computation.12 | async-start | bytes 4456448 | tf_op jit(solution)/shard_map/all_gather | solution.py:70
  81.0 2.2 copy-start.3
  94.0 97.5 %all-gather.12.cloned.1.call-start = ((), (), s32[]{:S(2)}) async-start(), calls=%async_computation.10 | async-start | bytes 4456448 | tf_op jit(solution)/shard_map/all_gather | solution.py:70
  95.6 2.3 copy-start.4
  110.0 130.7 %all-gather.10.cloned.1.call-start = ((), (), s32[]{:S(2)}) async-start(), calls=%async_computation.8 | async-start | bytes 4456448 | tf_op jit(solution)/shard_map/all_gather | solution.py:70
  110.4 3.6 copy-start.5
  124.2 165.7 %all-gather.8.cloned.1.call-start = ((), (), s32[]{:S(2)}) async-start(), calls=%async_computation.6 | async-start | bytes 4456448 | tf_op jit(solution)/shard_map/all_gather | solution.py:70
  124.5 3.2 copy-start.6
  137.2 185.1 %reduce-scatter.11.cloned.1.call-start = ((), (), s32[]{:S(2)}) async-start(), calls=%async_computation.13 | async-start | bytes 2621440 | tf_op jit(solution)/shard_map/reduce_scatter | solution.py:72
  147.9 209.1 %reduce-scatter.9.cloned.1.call-start = ((), (), s32[]{:S(2)}) async-start(), calls=%async_computation.11 | async-start | bytes 2621440 | tf_op jit(solution)/shard_map/reduce_scatter | solution.py:72
  197.4 194.2 %reduce-scatter.7.cloned.1.call-start = ((), (), s32[]{:S(2)}) async-start(), calls=%async_computation.9 | async-start | bytes 2621440 | tf_op jit(solution)/shard_map/reduce_scatter | solution.py:72
  246.6 179.6 %copy-start.2 = (bf16[1024,512]{1,0:T(8,128)(2,1)S(1)}, bf16[1024,512]{1,0:T(8,128)(2,1)}, u32[]{:S(2)}) copy-start(bf16[1024,512]{1,0:T(8,128)(2,1)} %param.8) | copy-start | bytes 3145732
  246.6 179.6 %reduce-scatter.5.cloned.1.call-start = ((), (), s32[]{:S(2)}) async-start(), calls=%async_computation.7 | async-start | bytes 2621440 | tf_op jit(solution)/shard_map/reduce_scatter | solution.py:72
Sparse Core Ops, SparseCore 0:
  9.2 64.9 all-gather.5
  94.2 47.7 all-gather.13
  143.8 47.6 all-gather.11
  193.1 47.5 all-gather.9
  242.3 47.5 all-gather.7
  292.3 30.0 reduce-scatter.10
  324.9 31.9 reduce-scatter.8
  359.5 31.9 reduce-scatter.6
  394.1 32.0 reduce-scatter.4
where the time goes:
time: 440 us; the launch traced here: 436 us
  waiting for transfers between devices  299 us (68%)
  matrix products  62.2 us (14%)
  other arithmetic  33.2 us (8%)
  local copies, waits for them, and re-layouts  15.3 us (3%)
  between operations  14.2 us (3%)
  starting transfers between devices  11.8 us (3%)
    all_gather x4, waiting for transfers between devices, on_device(): gathered = lax.all_gather(chunk_heads, 'seq', axis=1, tiled=True)  135 us
    reduce_scatter x4, waiting for transfers between devices, on_device(): lax.psum_scatter(projected, 'tensor', scatter_dimension=0, tiled=True)  130 us
    all_to_all x1, waiting for transfers between devices, on_device(): lax.all_to_all(query_slab, 'seq', split_axis=2, concat_axis=0, tiled=True)  34.3 us
    dot_general x4, matrix products, on_device(): jnp.dot(gathered, out_weight, preferred_element_type=jnp.float32)  23.4 us
    dot_general x16, matrix products, attend_rows(): jnp.einsum('qk,kd->qd', weights, value_head[:key_end], preferred_element_...  21 us
    dot_general x16, matrix products, attend_rows(): jnp.einsum('qd,kd->qk', query_block, key_head[:key_end], preferred_elemen...  17.8 us
    reduce_sum x16, other arithmetic, attend_rows(): jnp.sum(exponents, axis=-1, keepdims=True)  15.8 us
    unnamed x1, other arithmetic  11.6 us
  transfers between devices with their start and end apart: 10, of which 9 were waited for; matrix products, arithmetic and copies ran while one was open for 21% of the time, Pallas kernels for 0%

commit v1 on v0

--- a/solution.py
+++ b/solution.py
@@ -9,6 +9,12 @@
 HD = 128
 L = 4096
 CHUNKS = 4
+
+
+def in_order(parts, dim):
+    parts = jnp.moveaxis(parts, 0, dim)
+    shape = parts.shape
+    return parts.reshape(*shape[:dim], shape[dim] * shape[dim + 1], *shape[dim + 2 :])
 
 
 def attend_rows(query_head, key_head, value_head, doc_ids, first_row, rows):
@@ -67,7 +73,19 @@
             for part in range(n_ten)
         ]
         chunk_heads = jnp.concatenate(blocks, axis=0)
-        gathered = lax.all_gather(chunk_heads, "seq", axis=1, tiled=True)
+        count = lax.axis_size("seq")
+        pairs = [(i, (i + 1) % count) for i in range(count)]
+        back = [(b, a) for a, b in pairs]
+        lower, upper = ([], [])
+        for lap in range(count - 1):
+            if lap % 2 == 0:
+                lower.append(lax.ppermute(lower[-1] if lower else chunk_heads, "seq", pairs))
+            else:
+                upper.append(lax.ppermute(upper[-1] if upper else chunk_heads, "seq", back))
+        blocks_2 = jnp.stack([*lower[::-1], chunk_heads, *upper])
+        shift = lax.axis_index("seq") - len(lower)
+        blocks_2 = blocks_2[(jnp.arange(count) - shift) % count]
+        gathered = in_order(blocks_2, 1)
         projected = jnp.dot(gathered, out_weight, preferred_element_type=jnp.float32)
         pieces.append(lax.psum_scatter(projected, "tensor", scatter_dimension=0, tiled=True))
     summed = jnp.concatenate(pieces, axis=0)

time: 440 us -> 424 us (0.964)
  waiting for transfers between devices: 299 us -> 105 us
  local copies, waits for them, and re-layouts: 15.3 us -> 133 us
  starting transfers between devices: 11.8 us -> 72.7 us
  matrix products: 62.2 us -> 57 us
    all_gather x4 -> x0, waiting for transfers between devices: 135 us -> none  [on_device(): gathered = lax.all_gather(chunk_heads, 'seq', axis=1, tiled=True)]
    reduce_scatter x4, waiting for transfers between devices: 130 us -> 32.2 us  [on_device(): lax.psum_scatter(projected, 'tensor', scatter_dimension=0, tiled=True)]
    unnamed x19 -> x193, local copies, waits for them, and re-layouts: 9.34 us -> 74.7 us
    ppermute x0 -> x60, starting transfers between devices: none -> 62.2 us  [the longest x28 42.7 us: on_device(): upper.append(lax.ppermute(upper[-1] if upper else chunk_heads, 'seq', back))]
    ppermute x0 -> x60, waiting for transfers between devices: none -> 40.9 us  [the longest x32 28.1 us: on_device(): lax.ppermute(lower[-1] if lower else chunk_heads, 'seq', pairs)]
    transpose x0 -> x4, local copies, waits for them, and re-layouts: none -> 25.6 us  [in_order(): parts = jnp.moveaxis(parts, 0, dim)]
    gather x0 -> x4, local copies, waits for them, and re-layouts: none -> 21.8 us  [on_device(): blocks_2 = blocks_2[(jnp.arange(count) - shift) % count]]
    dot_general x16, matrix products: 17.8 us -> 12.8 us  [attend_rows(): jnp.einsum('qd,kd->qk', query_block, key_head[:key_end], preferred_elemen...]
  transfers between devices with their start and end apart: 10 -> 66, of which waited for: 9 -> 20; matrix products, arithmetic and copies ran while one was open for 21% -> 49% of each run, Pallas kernels for 0% -> 0%
where the time goes in v1:
time: 424 us; the launch traced here: 419 us
  local copies, waits for them, and re-layouts  133 us (31%)
  waiting for transfers between devices  105 us (25%)
  starting transfers between devices  72.7 us (17%)
  matrix products  57 us (13%)
  other arithmetic  35.9 us (8%)
  between operations  14.4 us (3%)
    unnamed x193, local copies, waits for them, and re-layouts  74.7 us
    ppermute x28, starting transfers between devices, on_device(): upper.append(lax.ppermute(upper[-1] if upper else chunk_heads, 'seq', back))  42.7 us
    reduce_scatter x4, waiting for transfers between devices, on_device(): lax.psum_scatter(projected, 'tensor', scatter_dimension=0, tiled=True)  32.2 us
    all_to_all x1, waiting for transfers between devices, on_device(): lax.all_to_all(query_slab, 'seq', split_axis=2, concat_axis=0, tiled=True)  32.1 us
    ppermute x32, waiting for transfers between devices, on_device(): lax.ppermute(lower[-1] if lower else chunk_heads, 'seq', pairs)  28.1 us
    transpose x4, local copies, waits for them, and re-layouts, in_order(): parts = jnp.moveaxis(parts, 0, dim)  25.6 us
    dot_general x4, matrix products, on_device(): jnp.dot(gathered, out_weight, preferred_element_type=jnp.float32)  23.7 us
    gather x4, local copies, waits for them, and re-layouts, on_device(): blocks_2 = blocks_2[(jnp.arange(count) - shift) % count]  21.8 us
  transfers between devices with their start and end apart: 66, of which 20 were waited for; matrix products, arithmetic and copies ran while one was open for 49% of the time, Pallas kernels for 0%

profile of v1, /device:TPU:1, one launch (start us, length us, event | category | flops | bytes accessed | tf_op | source)
XLA Modules:
  0.0 418.8 jit_solution(1755210666393819706)
XLA Ops:
  6.5 1.8 copy.55
  8.4 6.0 %copy.56 = bf16[256,1,2048]{0,1,2:T(2,128)(2,1)} copy(bf16[256,1,2048]{2,0,1:T(8,128)(2,1)} %bitcast.462) | data formatting | bytes 2097152 | tf_op jit(solution)/shard_map/reshape | solution.py:49
  14.9 11.6 %reduce = bf16[2048,256]{1,0:T(8,128)(2,1)S(1)} reduce(bf16[2048,1,256]{2,1,0:T(2,128)(2,1)} %bitcast.452, bf16[]{:T(256)} %broadcast.250), dimensions={1}, to_apply=%bitcast.366.reduce_sub_computation | reduce | bytes 2097154
  27.6 10.0 %all-to-all-start = ((bf16[16,2,16384]{2,1,0:T(2,128)(2,1)}), bf16[16,2,16384]{2,1,0:T(2,128)(2,1)S(1)}, u32[]{:S(2)}, u32[]{:S(2)}) async-start(bf16[16,2,16384]{2,1,0:T(2,128)(2,1)} %reshape.288), calls=%async_computation | async-start | bytes 2097152 | tf_op jit(solution)/shard_map/all_to_all | solution.py:50
  40.5 32.1 %all-to-all-done = bf16[16,2,16384]{2,1,0:T(2,128)(2,1)S(1)} async-done(((bf16[16,2,16384]{2,1,0:T(2,128)(2,1)}), bf16[16,2,16384]{2,1,0:T(2,128)(2,1)S(1)}, u32[]{:S(2)}, u32[]{:S(2)}) %all-to-all-start) | async-done | bytes 1048608 | tf_op jit(solution)/shard_map/all_to_all | solution.py:50
  72.5 3.5 reshape.289
  76.0 1.8 copy.77
  77.8 3.2 fusion.132
  81.0 1.9 fusion.30
  87.6 2.3 fusion.65
  95.0 2.1 fusion.32
  101.3 2.2 fusion.64
  115.9 2.0 fusion.63
  124.4 1.9 fusion.70
  127.1 2.6 collective-permute-done.46
  129.7 2.5 collective-permute-start.47
  133.5 2.8 collective-permute-done.47
  137.9 1.9 fusion.66
  139.9 3.4 collective-permute-done.48
  144.4 5.9 %collective-permute-done.49 = bf16[1024,128]{1,0:T(8,128)(2,1)S(1)} collective-permute-done((bf16[1024,128]{1,0:T(8,128)(2,1)S(1)}, bf16[1024,128]{1,0:T(8,128)(2,1)S(1)}, u32[]{:S(2)}, u32[]{:S(2)}) %collective-permute-start.49) | collective-permute-done | bytes 262176 | tf_op jit(solution)/shard_map/ppermute | solution.py:82
  150.8 6.5 %collective-permute-done.50 = bf16[1024,128]{1,0:T(8,128)(2,1)S(1)} collective-permute-done((bf16[1024,128]{1,0:T(8,128)(2,1)S(1)}, bf16[1024,128]{1,0:T(8,128)(2,1)S(1)}, u32[]{:S(2)}, u32[]{:S(2)}) %collective-permute-start.50) | collective-permute-done | bytes 262176 | tf_op jit(solution)/shard_map/ppermute | solution.py:82
  158.0 6.3 %collective-permute-done.51 = bf16[1024,128]{1,0:T(8,128)(2,1)S(1)} collective-permute-done((bf16[1024,128]{1,0:T(8,128)(2,1)S(1)}, bf16[1024,128]{1,0:T(8,128)(2,1)S(1)}, u32[]{:S(2)}, u32[]{:S(2)}) %collective-permute-start.51) | collective-permute-done | bytes 262176 | tf_op jit(solution)/shard_map/ppermute | solution.py:82
  164.7 6.0 %collective-permute-start.23 = (bf16[1024,128]{1,0:T(8,128)(2,1)S(1)}, bf16[1024,128]{1,0:T(8,128)(2,1)S(1)}, u32[]{:S(2)}, u32[]{:S(2)}) collective-permute-start(bf16[1024,128]{1,0:T(8,128)(2,1)S(1)} %pad_maximum_fusion.1), channel_id=1, source_target_pairs={{4,0},{8,4},{12,8},{16,12},{20,16},{24,20},{28,24},{32,28},{36,32}... | collective-permute-start | bytes 786440 | tf_op jit(solution)/shard_map/ppermute | solution.py:84
  171.3 6.0 %collective-permute-start.8 = (bf16[1024,128]{1,0:T(8,128)(2,1)S(1)}, bf16[1024,128]{1,0:T(8,128)(2,1)S(1)}, u32[]{:S(2)}, u32[]{:S(2)}) collective-permute-start(bf16[1024,128]{1,0:T(8,128)(2,1)S(1)} %pad_maximum_fusion), channel_id=1, source_target_pairs={{4,0},{8,4},{12,8},{16,12},{20,16},{24,20},{28,24},{32,28},{36,32}... | collective-permute-start | bytes 786440 | tf_op jit(solution)/shard_map/ppermute | solution.py:84
  204.2 2.0 collective-permute-start.26
  207.3 1.9 collective-permute-start.57
  212.8 1.9 collective-permute-start.42
  215.8 1.8 collective-permute-start.58
  221.3 2.6 collective-permute-done.58
  225.8 3.1 collective-permute-start.12
  232.2 5.4 %gather_fusion.3 = bf16[16,1024,128]{2,1,0:T(8,128)(2,1)} fusion(bf16[16,1024,128]{2,1,0:T(8,128)(2,1)} %bitcast_dynamic-update-slice_fusion, s32[1024]{0:T(1024)} %pad_clamp_fusion), kind=kCustom, calls=%fused_computation.3 | custom fusion | bytes 8388672 | tf_op jit(solution)/shard_map/gather | solution.py:87
  237.7 6.4 %copy.76 = bf16[1024,16,128]{0,2,1:T(8,128)(2,1)} copy(bf16[1024,16,128]{2,0,1:T(8,128)(2,1)} %bitcast.445) | data formatting | bytes 8388608 | tf_op jit(solution)/shard_map/transpose | solution.py:15
  244.1 2.6 collective-permute-start.28
  246.7 2.9 collective-permute-start.13
  249.7 5.9 %fusion.151 = f32[1024,512]{1,0:T(8,128)} fusion(bf16[1024,2048]{0,1:T(8,128)(2,1)} %bitcast.443, bf16[2048,512]{1,0:T(8,128)(2,1)S(1)} %copy-done), kind=kOutput, calls=%fused_computation.364 | convolution fusion | flops 2147483648 | bytes 8388608 | tf_op jit(solution)/shard_map/dot_general | solution.py:89
  256.2 2.9 collective-permute-start.29
  281.6 5.4 %gather_fusion.2 = bf16[16,1024,128]{2,1,0:T(8,128)(2,1)} fusion(bf16[16,1024,128]{2,1,0:T(8,128)(2,1)} %bitcast_dynamic-update-slice_fusion.16, s32[1024]{0:T(1024)} %pad_clamp_fusion), kind=kCustom, calls=%fused_computation.2 | custom fusion | bytes 8388672 | tf_op jit(solution)/shard_map/gather | solution.py:87
  287.0 6.4 %copy.71 = bf16[1024,16,128]{0,2,1:T(8,128)(2,1)} copy(bf16[1024,16,128]{2,0,1:T(8,128)(2,1)} %bitcast.446) | data formatting | bytes 8388608 | tf_op jit(solution)/shard_map/transpose | solution.py:15
  293.4 6.0 %fusion.150 = f32[1024,512]{1,0:T(8,128)} fusion(bf16[1024,2048]{0,1:T(8,128)(2,1)} %bitcast.447, bf16[2048,512]{1,0:T(8,128)(2,1)S(1)} %copy-done), kind=kOutput, calls=%fused_computation.363 | convolution fusion | flops 2147483648 | bytes 8388608 | tf_op jit(solution)/shard_map/dot_general | solution.py:89
  320.9 5.5 %gather_fusion.1 = bf16[16,1024,128]{2,1,0:T(8,128)(2,1)} fusion(bf16[16,1024,128]{2,1,0:T(8,128)(2,1)} %bitcast_dynamic-update-slice_fusion.32, s32[1024]{0:T(1024)} %pad_clamp_fusion), kind=kCustom, calls=%fused_computation.1 | custom fusion | bytes 8388672 | tf_op jit(solution)/shard_map/gather | solution.py:87
  326.4 6.4 %copy.66 = bf16[1024,16,128]{0,2,1:T(8,128)(2,1)} copy(bf16[1024,16,128]{2,0,1:T(8,128)(2,1)} %bitcast.448) | data formatting | bytes 8388608 | tf_op jit(solution)/shard_map/transpose | solution.py:15
  332.8 5.9 %fusion.149 = f32[1024,512]{1,0:T(8,128)} fusion(bf16[1024,2048]{0,1:T(8,128)(2,1)} %bitcast.449, bf16[2048,512]{1,0:T(8,128)(2,1)S(1)} %copy-done), kind=kOutput, calls=%fused_computation.362 | convolution fusion | flops 2147483648 | bytes 8388608 | tf_op jit(solution)/shard_map/dot_general | solution.py:89
  338.8 1.8 bitcast_dynamic-update-slice_fusion.63
  359.0 5.5 %gather_fusion = bf16[16,1024,128]{2,1,0:T(8,128)(2,1)} fusion(bf16[16,1024,128]{2,1,0:T(8,128)(2,1)} %bitcast_dynamic-update-slice_fusion.48, s32[1024]{0:T(1024)} %pad_clamp_fusion), kind=kCustom, calls=%fused_computation | custom fusion | bytes 8388672 | tf_op jit(solution)/shard_map/gather | solution.py:87
  364.5 6.4 %copy.61 = bf16[1024,16,128]{0,2,1:T(8,128)(2,1)} copy(bf16[1024,16,128]{2,0,1:T(8,128)(2,1)} %bitcast.444) | data formatting | bytes 8388608 | tf_op jit(solution)/shard_map/transpose | solution.py:15
  370.9 6.0 %fusion.148 = f32[1024,512]{1,0:T(8,128)} fusion(bf16[1024,2048]{0,1:T(8,128)(2,1)} %bitcast.450, bf16[2048,512]{1,0:T(8,128)(2,1)S(1)} %copy-done), kind=kOutput, calls=%fused_computation.361 | convolution fusion | flops 2147483648 | bytes 8388608 | tf_op jit(solution)/shard_map/dot_general | solution.py:89
  377.0 32.2 %reduce-scatter.5.cloned.1.call-done = f32[256,512]{1,0:T(8,128)} async-done(((f32[1024,512]{1,0:T(8,128)}), f32[256,512]{1,0:T(8,128)}) %reduce-scatter.5.cloned.1.call-update) | async-done | bytes 524304 | tf_op jit(solution)/shard_map/reduce_scatter | solution.py:90
  409.2 2.8 fusion.36
  (385 shorter events, 148.6 us)
Async XLA Ops:
  6.5 71.3 %all-gather.2.cloned.1.call-start = ((), (), s32[]{:S(2)}) async-start(), calls=%async_computation.5 | async-start | bytes 4456448 | tf_op jit(solution)/shard_map/all_gather | solution.py:54
  27.6 44.9 %all-to-all-start = ((bf16[16,2,16384]{2,1,0:T(2,128)(2,1)}), bf16[16,2,16384]{2,1,0:T(2,128)(2,1)S(1)}, u32[]{:S(2)}, u32[]{:S(2)}) async-start(bf16[16,2,16384]{2,1,0:T(2,128)(2,1)} %reshape.288), calls=%async_computation | async-start | bytes 2097152 | tf_op jit(solution)/shard_map/all_to_all | solution.py:50
  37.6 339.3 %reduce-scatter.11.cloned.1.call-start = ((), (), s32[]{:S(2)}) async-start(), calls=%async_computation.9 | async-start | bytes 2621440 | tf_op jit(solution)/shard_map/reduce_scatter | solution.py:90
  93.4 32.9 %collective-permute-start.45 = (bf16[1024,128]{1,0:T(8,128)(2,1)S(1)}, bf16[1024,128]{1,0:T(8,128)(2,1)S(1)}, u32[]{:S(2)}, u32[]{:S(2)}) collective-permute-start(bf16[1024,128]{1,0:T(8,128)(2,1)S(1)} %pad_maximum_fusion.3), channel_id=1, source_target_pairs={{0,4},{4,8},{8,12},{12,16},{16,20},{20,24},{24,28},{28,32},{32,36}... | collective-permute-start | bytes 786440 | tf_op jit(solution)/shard_map/ppermute | solution.py:82
  93.9 70.8 %collective-permute-start.53 = (bf16[1024,128]{1,0:T(8,128)(2,1)S(1)}, bf16[1024,128]{1,0:T(8,128)(2,1)S(1)}, u32[]{:S(2)}, u32[]{:S(2)}) collective-permute-start(bf16[1024,128]{1,0:T(8,128)(2,1)S(1)} %pad_maximum_fusion.3), channel_id=1, source_target_pairs={{4,0},{8,4},{12,8},{16,12},{20,16},{24,20},{28,24},{32,28},{36,32}... | collective-permute-start | bytes 786440 | tf_op jit(solution)/shard_map/ppermute | solution.py:84
  106.7 64.0 %collective-permute-start.30 = (bf16[1024,128]{1,0:T(8,128)(2,1)S(1)}, bf16[1024,128]{1,0:T(8,128)(2,1)S(1)}, u32[]{:S(2)}, u32[]{:S(2)}) collective-permute-start(bf16[1024,128]{1,0:T(8,128)(2,1)S(1)} %pad_maximum_fusion.2), channel_id=1, source_target_pairs={{0,4},{4,8},{8,12},{12,16},{16,20},{20,24},{24,28},{28,32},{32,36}... | collective-permute-start | bytes 786440 | tf_op jit(solution)/shard_map/ppermute | solution.py:82
  108.4 70.3 %collective-permute-start.38 = (bf16[1024,128]{1,0:T(8,128)(2,1)S(1)}, bf16[1024,128]{1,0:T(8,128)(2,1)S(1)}, u32[]{:S(2)}, u32[]{:S(2)}) collective-permute-start(bf16[1024,128]{1,0:T(8,128)(2,1)S(1)} %pad_maximum_fusion.2), channel_id=1, source_target_pairs={{4,0},{8,4},{12,8},{16,12},{20,16},{24,20},{28,24},{32,28},{36,32}... | collective-permute-start | bytes 786440 | tf_op jit(solution)/shard_map/ppermute | solution.py:84
  120.8 58.0 %collective-permute-start.15 = (bf16[1024,128]{1,0:T(8,128)(2,1)S(1)}, bf16[1024,128]{1,0:T(8,128)(2,1)S(1)}, u32[]{:S(2)}, u32[]{:S(2)}) collective-permute-start(bf16[1024,128]{1,0:T(8,128)(2,1)S(1)} %pad_maximum_fusion.1), channel_id=1, source_target_pairs={{0,4},{4,8},{8,12},{12,16},{16,20},{20,24},{24,28},{28,32},{32,36}... | collective-permute-start | bytes 786440 | tf_op jit(solution)/shard_map/ppermute | solution.py:82
  164.7 15.8 %collective-permute-start.23 = (bf16[1024,128]{1,0:T(8,128)(2,1)S(1)}, bf16[1024,128]{1,0:T(8,128)(2,1)S(1)}, u32[]{:S(2)}, u32[]{:S(2)}) collective-permute-start(bf16[1024,128]{1,0:T(8,128)(2,1)S(1)} %pad_maximum_fusion.1), channel_id=1, source_target_pairs={{4,0},{8,4},{12,8},{16,12},{20,16},{24,20},{28,24},{32,28},{36,32}... | collective-permute-start | bytes 786440 | tf_op jit(solution)/shard_map/ppermute | solution.py:84
  170.7 9.8 %collective-permute-start = (bf16[1024,128]{1,0:T(8,128)(2,1)S(1)}, bf16[1024,128]{1,0:T(8,128)(2,1)S(1)}, u32[]{:S(2)}, u32[]{:S(2)}) collective-permute-start(bf16[1024,128]{1,0:T(8,128)(2,1)S(1)} %pad_maximum_fusion), channel_id=1, source_target_pairs={{0,4},{4,8},{8,12},{12,16},{16,20},{20,24},{24,28},{28,32},{32,36}... | collective-permute-start | bytes 786440 | tf_op jit(solution)/shard_map/ppermute | solution.py:82
  171.3 11.0 %collective-permute-start.8 = (bf16[1024,128]{1,0:T(8,128)(2,1)S(1)}, bf16[1024,128]{1,0:T(8,128)(2,1)S(1)}, u32[]{:S(2)}, u32[]{:S(2)}) collective-permute-start(bf16[1024,128]{1,0:T(8,128)(2,1)S(1)} %pad_maximum_fusion), channel_id=1, source_target_pairs={{4,0},{8,4},{12,8},{16,12},{20,16},{24,20},{28,24},{32,28},{36,32}... | collective-permute-start | bytes 786440 | tf_op jit(solution)/shard_map/ppermute | solution.py:84
  180.5 8.6 %collective-permute-start.16 = (bf16[1024,128]{1,0:T(8,128)(2,1)S(1)}, bf16[1024,128]{1,0:T(8,128)(2,1)S(1)}, u32[]{:S(2)}, u32[]{:S(2)}) collective-permute-start(bf16[1024,128]{1,0:T(8,128)(2,1)S(1)} %collective-permute-done.15), channel_id=1, source_target_pairs={{0,4},{4,8},{8,12},{12,16},{16,20},{20,24},{24,28},{28,32},{32,36}... | collective-permute-start | bytes 786440 | tf_op jit(solution)/shard_map/ppermute | solution.py:82
  185.5 8.2 %collective-permute-start.9 = (bf16[1024,128]{1,0:T(8,128)(2,1)S(1)}, bf16[1024,128]{1,0:T(8,128)(2,1)S(1)}, u32[]{:S(2)}, u32[]{:S(2)}) collective-permute-start(bf16[1024,128]{1,0:T(8,128)(2,1)S(1)} %collective-permute-done.8), channel_id=1, source_target_pairs={{4,0},{8,4},{12,8},{16,12},{20,16},{24,20},{28,24},{32,28},{36,32}... | collective-permute-start | bytes 786440 | tf_op jit(solution)/shard_map/ppermute | solution.py:84
  187.7 8.4 %collective-permute-start.55 = (bf16[1024,128]{1,0:T(8,128)(2,1)S(1)}, bf16[1024,128]{1,0:T(8,128)(2,1)S(1)}, u32[]{:S(2)}, u32[]{:S(2)}) collective-permute-start(bf16[1024,128]{1,0:T(8,128)(2,1)S(1)} %collective-permute-done.54), channel_id=1, source_target_pairs={{4,0},{8,4},{12,8},{16,12},{20,16},{24,20},{28,24},{32,28},{36,32}... | collective-permute-start | bytes 786440 | tf_op jit(solution)/shard_map/ppermute | solution.py:84
  190.5 8.4 %collective-permute-start.40 = (bf16[1024,128]{1,0:T(8,128)(2,1)S(1)}, bf16[1024,128]{1,0:T(8,128)(2,1)S(1)}, u32[]{:S(2)}, u32[]{:S(2)}) collective-permute-start(bf16[1024,128]{1,0:T(8,128)(2,1)S(1)} %collective-permute-done.39), channel_id=1, source_target_pairs={{4,0},{8,4},{12,8},{16,12},{20,16},{24,20},{28,24},{32,28},{36,32}... | collective-permute-start | bytes 786440 | tf_op jit(solution)/shard_map/ppermute | solution.py:84
  192.0 9.8 %collective-permute-start.17 = (bf16[1024,128]{1,0:T(8,128)(2,1)S(1)}, bf16[1024,128]{1,0:T(8,128)(2,1)S(1)}, u32[]{:S(2)}, u32[]{:S(2)}) collective-permute-start(bf16[1024,128]{1,0:T(8,128)(2,1)S(1)} %collective-permute-done.16), channel_id=1, source_target_pairs={{0,4},{4,8},{8,12},{12,16},{16,20},{20,24},{24,28},{28,32},{32,36}... | collective-permute-start | bytes 786440 | tf_op jit(solution)/shard_map/ppermute | solution.py:82
  193.7 8.4 %collective-permute-start.25 = (bf16[1024,128]{1,0:T(8,128)(2,1)S(1)}, bf16[1024,128]{1,0:T(8,128)(2,1)S(1)}, u32[]{:S(2)}, u32[]{:S(2)}) collective-permute-start(bf16[1024,128]{1,0:T(8,128)(2,1)S(1)} %collective-permute-done.24), channel_id=1, source_target_pairs={{4,0},{8,4},{12,8},{16,12},{20,16},{24,20},{28,24},{32,28},{36,32}... | collective-permute-start | bytes 786440 | tf_op jit(solution)/shard_map/ppermute | solution.py:84
  198.9 8.4 %collective-permute-start.56 = (bf16[1024,128]{1,0:T(8,128)(2,1)S(1)}, bf16[1024,128]{1,0:T(8,128)(2,1)S(1)}, u32[]{:S(2)}, u32[]{:S(2)}) collective-permute-start(bf16[1024,128]{1,0:T(8,128)(2,1)S(1)} %collective-permute-done.55), channel_id=1, source_target_pairs={{4,0},{8,4},{12,8},{16,12},{20,16},{24,20},{28,24},{32,28},{36,32}... | collective-permute-start | bytes 786440 | tf_op jit(solution)/shard_map/ppermute | solution.py:84
  201.8 8.9 %collective-permute-start.33 = (bf16[1024,128]{1,0:T(8,128)(2,1)S(1)}, bf16[1024,128]{1,0:T(8,128)(2,1)S(1)}, u32[]{:S(2)}, u32[]{:S(2)}) collective-permute-start(bf16[1024,128]{1,0:T(8,128)(2,1)S(1)} %collective-permute-done.32), channel_id=1, source_target_pairs={{0,4},{4,8},{8,12},{12,16},{16,20},{20,24},{24,28},{28,32},{32,36}... | collective-permute-start | bytes 786440 | tf_op jit(solution)/shard_map/ppermute | solution.py:82
  202.1 8.6 %collective-permute-start.41 = (bf16[1024,128]{1,0:T(8,128)(2,1)S(1)}, bf16[1024,128]{1,0:T(8,128)(2,1)S(1)}, u32[]{:S(2)}, u32[]{:S(2)}) collective-permute-start(bf16[1024,128]{1,0:T(8,128)(2,1)S(1)} %collective-permute-done.40), channel_id=1, source_target_pairs={{4,0},{8,4},{12,8},{16,12},{20,16},{24,20},{28,24},{32,28},{36,32}... | collective-permute-start | bytes 786440 | tf_op jit(solution)/shard_map/ppermute | solution.py:84
  203.3 8.4 %collective-permute-start.18 = (bf16[1024,128]{1,0:T(8,128)(2,1)S(1)}, bf16[1024,128]{1,0:T(8,128)(2,1)S(1)}, u32[]{:S(2)}, u32[]{:S(2)}) collective-permute-start(bf16[1024,128]{1,0:T(8,128)(2,1)S(1)} %collective-permute-done.17), channel_id=1, source_target_pairs={{0,4},{4,8},{8,12},{12,16},{16,20},{20,24},{24,28},{28,32},{32,36}... | collective-permute-start | bytes 786440 | tf_op jit(solution)/shard_map/ppermute | solution.py:82
  204.2 8.6 %collective-permute-start.26 = (bf16[1024,128]{1,0:T(8,128)(2,1)S(1)}, bf16[1024,128]{1,0:T(8,128)(2,1)S(1)}, u32[]{:S(2)}, u32[]{:S(2)}) collective-permute-start(bf16[1024,128]{1,0:T(8,128)(2,1)S(1)} %collective-permute-done.25), channel_id=1, source_target_pairs={{4,0},{8,4},{12,8},{16,12},{20,16},{24,20},{28,24},{32,28},{36,32}... | collective-permute-start | bytes 786440 | tf_op jit(solution)/shard_map/ppermute | solution.py:84
  207.3 8.4 %collective-permute-start.57 = (bf16[1024,128]{1,0:T(8,128)(2,1)S(1)}, bf16[1024,128]{1,0:T(8,128)(2,1)S(1)}, u32[]{:S(2)}, u32[]{:S(2)}) collective-permute-start(bf16[1024,128]{1,0:T(8,128)(2,1)S(1)} %collective-permute-done.56), channel_id=1, source_target_pairs={{4,0},{8,4},{12,8},{16,12},{20,16},{24,20},{28,24},{32,28},{36,32}... | collective-permute-start | bytes 786440 | tf_op jit(solution)/shard_map/ppermute | solution.py:84
  210.7 8.4 %collective-permute-start.3 = (bf16[1024,128]{1,0:T(8,128)(2,1)S(1)}, bf16[1024,128]{1,0:T(8,128)(2,1)S(1)}, u32[]{:S(2)}, u32[]{:S(2)}) collective-permute-start(bf16[1024,128]{1,0:T(8,128)(2,1)S(1)} %collective-permute-done.2), channel_id=1, source_target_pairs={{0,4},{4,8},{8,12},{12,16},{16,20},{20,24},{24,28},{28,32},{32,36}... | collective-permute-start | bytes 786440 | tf_op jit(solution)/shard_map/ppermute | solution.py:82
  210.7 8.3 %collective-permute-start.11 = (bf16[1024,128]{1,0:T(8,128)(2,1)S(1)}, bf16[1024,128]{1,0:T(8,128)(2,1)S(1)}, u32[]{:S(2)}, u32[]{:S(2)}) collective-permute-start(bf16[1024,128]{1,0:T(8,128)(2,1)S(1)} %collective-permute-done.10), channel_id=1, source_target_pairs={{4,0},{8,4},{12,8},{16,12},{20,16},{24,20},{28,24},{32,28},{36,32}... | collective-permute-start | bytes 786440 | tf_op jit(solution)/shard_map/ppermute | solution.py:84
  211.7 8.8 %collective-permute-start.34 = (bf16[1024,128]{1,0:T(8,128)(2,1)S(1)}, bf16[1024,128]{1,0:T(8,128)(2,1)S(1)}, u32[]{:S(2)}, u32[]{:S(2)}) collective-permute-start(bf16[1024,128]{1,0:T(8,128)(2,1)S(1)} %collective-permute-done.33), channel_id=1, source_target_pairs={{0,4},{4,8},{8,12},{12,16},{16,20},{20,24},{24,28},{28,32},{32,36}... | collective-permute-start | bytes 786440 | tf_op jit(solution)/shard_map/ppermute | solution.py:82
  212.8 8.4 %collective-permute-start.42 = (bf16[1024,128]{1,0:T(8,128)(2,1)S(1)}, bf16[1024,128]{1,0:T(8,128)(2,1)}, u32[]{:S(2)}, u32[]{:S(2)}) collective-permute-start(bf16[1024,128]{1,0:T(8,128)(2,1)S(1)} %collective-permute-done.41), channel_id=1, source_target_pairs={{4,0},{8,4},{12,8},{16,12},{20,16},{24,20},{28,24},{32,28},{36,32}... | collective-permute-start | bytes 786440 | tf_op jit(solution)/shard_map/ppermute | solution.py:84
  219.1 9.8 %collective-permute-start.27 = (bf16[1024,128]{1,0:T(8,128)(2,1)S(1)}, bf16[1024,128]{1,0:T(8,128)(2,1)}, u32[]{:S(2)}, u32[]{:S(2)}) collective-permute-start(bf16[1024,128]{1,0:T(8,128)(2,1)S(1)} %collective-permute-done.26), channel_id=1, source_target_pairs={{4,0},{8,4},{12,8},{16,12},{20,16},{24,20},{28,24},{32,28},{36,32}... | collective-permute-start | bytes 786440 | tf_op jit(solution)/shard_map/ppermute | solution.py:84
  220.5 8.5 %collective-permute-start.4 = (bf16[1024,128]{1,0:T(8,128)(2,1)S(1)}, bf16[1024,128]{1,0:T(8,128)(2,1)}, u32[]{:S(2)}, u32[]{:S(2)}) collective-permute-start(bf16[1024,128]{1,0:T(8,128)(2,1)S(1)} %collective-permute-done.3), channel_id=1, source_target_pairs={{0,4},{4,8},{8,12},{12,16},{16,20},{20,24},{24,28},{28,32},{32,36}... | collective-permute-start | bytes 786440 | tf_op jit(solution)/shard_map/ppermute | solution.py:82
  221.3 9.4 %collective-permute-start.35 = (bf16[1024,128]{1,0:T(8,128)(2,1)S(1)}, bf16[1024,128]{1,0:T(8,128)(2,1)}, u32[]{:S(2)}, u32[]{:S(2)}) collective-permute-start(bf16[1024,128]{1,0:T(8,128)(2,1)S(1)} %collective-permute-done.34), channel_id=1, source_target_pairs={{0,4},{4,8},{8,12},{12,16},{16,20},{20,24},{24,28},{28,32},{32,36}... | collective-permute-start | bytes 786440 | tf_op jit(solution)/shard_map/ppermute | solution.py:82
  225.8 18.3 %collective-permute-start.12 = (bf16[1024,128]{1,0:T(8,128)(2,1)S(1)}, bf16[1024,128]{1,0:T(8,128)(2,1)}, u32[]{:S(2)}, u32[]{:S(2)}) collective-permute-start(bf16[1024,128]{1,0:T(8,128)(2,1)S(1)} %collective-permute-done.11), channel_id=1, source_target_pairs={{4,0},{8,4},{12,8},{16,12},{20,16},{24,20},{28,24},{32,28},{36,32}... | collective-permute-start | bytes 786440 | tf_op jit(solution)/shard_map/ppermute | solution.py:84
  228.9 17.8 %collective-permute-start.43 = (bf16[1024,128]{1,0:T(8,128)(2,1)}, bf16[1024,128]{1,0:T(8,128)(2,1)}, u32[]{:S(2)}, u32[]{:S(2)}) collective-permute-start(bf16[1024,128]{1,0:T(8,128)(2,1)} %collective-permute-done.42), channel_id=1, source_target_pairs={{4,0},{8,4},{12,8},{16,12},{20,16},{24,20},{28,24},{32,28},{36,32}... | collective-permute-start | bytes 786440 | tf_op jit(solution)/shard_map/ppermute | solution.py:84
  229.0 20.7 %collective-permute-start.20 = (bf16[1024,128]{1,0:T(8,128)(2,1)}, bf16[1024,128]{1,0:T(8,128)(2,1)}, u32[]{:S(2)}, u32[]{:S(2)}) collective-permute-start(bf16[1024,128]{1,0:T(8,128)(2,1)} %collective-permute-done.19), channel_id=1, source_target_pairs={{0,4},{4,8},{8,12},{12,16},{16,20},{20,24},{24,28},{28,32},{32,36}... | collective-permute-start | bytes 786440 | tf_op jit(solution)/shard_map/ppermute | solution.py:82
  230.7 18.9 %collective-permute-start.5 = (bf16[1024,128]{1,0:T(8,128)(2,1)}, bf16[1024,128]{1,0:T(8,128)(2,1)}, u32[]{:S(2)}, u32[]{:S(2)}) collective-permute-start(bf16[1024,128]{1,0:T(8,128)(2,1)} %collective-permute-done.4), channel_id=1, source_target_pairs={{0,4},{4,8},{8,12},{12,16},{16,20},{20,24},{24,28},{28,32},{32,36}... | collective-permute-start | bytes 786440 | tf_op jit(solution)/shard_map/ppermute | solution.py:82
  230.7 18.9 %collective-permute-start.36 = (bf16[1024,128]{1,0:T(8,128)(2,1)}, bf16[1024,128]{1,0:T(8,128)(2,1)}, u32[]{:S(2)}, u32[]{:S(2)}) collective-permute-start(bf16[1024,128]{1,0:T(8,128)(2,1)} %collective-permute-done.35), channel_id=1, source_target_pairs={{0,4},{4,8},{8,12},{12,16},{16,20},{20,24},{24,28},{28,32},{32,36}... | collective-permute-start | bytes 786440 | tf_op jit(solution)/shard_map/ppermute | solution.py:82
  244.1 11.7 %collective-permute-start.28 = (bf16[1024,128]{1,0:T(8,128)(2,1)}, bf16[1024,128]{1,0:T(8,128)(2,1)}, u32[]{:S(2)}, u32[]{:S(2)}) collective-permute-start(bf16[1024,128]{1,0:T(8,128)(2,1)} %collective-permute-done.27), channel_id=1, source_target_pairs={{4,0},{8,4},{12,8},{16,12},{20,16},{24,20},{28,24},{32,28},{36,32}... | collective-permute-start | bytes 786440 | tf_op jit(solution)/shard_map/ppermute | solution.py:84
  246.7 9.6 %collective-permute-start.13 = (bf16[1024,128]{1,0:T(8,128)(2,1)}, bf16[1024,128]{1,0:T(8,128)(2,1)}, u32[]{:S(2)}, u32[]{:S(2)}) collective-permute-start(bf16[1024,128]{1,0:T(8,128)(2,1)} %collective-permute-done.12), channel_id=1, source_target_pairs={{4,0},{8,4},{12,8},{16,12},{20,16},{24,20},{28,24},{32,28},{36,32}... | collective-permute-start | bytes 786440 | tf_op jit(solution)/shard_map/ppermute | solution.py:84
  249.6 9.6 %collective-permute-start.21 = (bf16[1024,128]{1,0:T(8,128)(2,1)}, bf16[1024,128]{1,0:T(8,128)(2,1)}, u32[]{:S(2)}, u32[]{:S(2)}) collective-permute-start(bf16[1024,128]{1,0:T(8,128)(2,1)} %collective-permute-done.20), channel_id=1, source_target_pairs={{0,4},{4,8},{8,12},{12,16},{16,20},{20,24},{24,28},{28,32},{32,36}... | collective-permute-start | bytes 786440 | tf_op jit(solution)/shard_map/ppermute | solution.py:82
  249.6 10.1 %collective-permute-start.6 = (bf16[1024,128]{1,0:T(8,128)(2,1)}, bf16[1024,128]{1,0:T(8,128)(2,1)}, u32[]{:S(2)}, u32[]{:S(2)}) collective-permute-start(bf16[1024,128]{1,0:T(8,128)(2,1)} %collective-permute-done.5), channel_id=1, source_target_pairs={{0,4},{4,8},{8,12},{12,16},{16,20},{20,24},{24,28},{28,32},{32,36}... | collective-permute-start | bytes 786440 | tf_op jit(solution)/shard_map/ppermute | solution.py:82
  249.7 11.3 %collective-permute-start.37 = (bf16[1024,128]{1,0:T(8,128)(2,1)}, bf16[1024,128]{1,0:T(8,128)(2,1)}, u32[]{:S(2)}, u32[]{:S(2)}) collective-permute-start(bf16[1024,128]{1,0:T(8,128)(2,1)} %collective-permute-done.36), channel_id=1, source_target_pairs={{0,4},{4,8},{8,12},{12,16},{16,20},{20,24},{24,28},{28,32},{32,36}... | collective-permute-start | bytes 786440 | tf_op jit(solution)/shard_map/ppermute | solution.py:82
  255.6 121.4 %reduce-scatter.9.cloned.1.call-start = ((), (), s32[]{:S(2)}) async-start(), calls=%async_computation.8 | async-start | bytes 2621440 | tf_op jit(solution)/shard_map/reduce_scatter | solution.py:90
  255.7 25.1 %collective-permute-start.44 = (bf16[1024,128]{1,0:T(8,128)(2,1)}, bf16[1024,128]{1,0:T(8,128)(2,1)S(1)}, u32[]{:S(2)}, u32[]{:S(2)}) collective-permute-start(bf16[1024,128]{1,0:T(8,128)(2,1)} %collective-permute-done.43), channel_id=1, source_target_pairs={{4,0},{8,4},{12,8},{16,12},{20,16},{24,20},{28,24},{32,28},{36,32}... | collective-permute-start | bytes 786440 | tf_op jit(solution)/shard_map/ppermute | solution.py:84
  256.2 63.0 %collective-permute-start.29 = (bf16[1024,128]{1,0:T(8,128)(2,1)}, bf16[1024,128]{1,0:T(8,128)(2,1)}, u32[]{:S(2)}, u32[]{:S(2)}) collective-permute-start(bf16[1024,128]{1,0:T(8,128)(2,1)} %collective-permute-done.28), channel_id=1, source_target_pairs={{4,0},{8,4},{12,8},{16,12},{20,16},{24,20},{28,24},{32,28},{36,32}... | collective-permute-start | bytes 786440 | tf_op jit(solution)/shard_map/ppermute | solution.py:84
  259.2 98.2 %collective-permute-start.14 = (bf16[1024,128]{1,0:T(8,128)(2,1)}, bf16[1024,128]{1,0:T(8,128)(2,1)}, u32[]{:S(2)}, u32[]{:S(2)}) collective-permute-start(bf16[1024,128]{1,0:T(8,128)(2,1)} %collective-permute-done.13), channel_id=1, source_target_pairs={{4,0},{8,4},{12,8},{16,12},{20,16},{24,20},{28,24},{32,28},{36,32}... | collective-permute-start | bytes 786440 | tf_op jit(solution)/shard_map/ppermute | solution.py:84
  259.7 40.0 %collective-permute-start.22 = (bf16[1024,128]{1,0:T(8,128)(2,1)}, bf16[1024,128]{1,0:T(8,128)(2,1)}, u32[]{:S(2)}, u32[]{:S(2)}) collective-permute-start(bf16[1024,128]{1,0:T(8,128)(2,1)} %collective-permute-done.21), channel_id=1, source_target_pairs={{0,4},{4,8},{8,12},{12,16},{16,20},{20,24},{24,28},{28,32},{32,36}... | collective-permute-start | bytes 786440 | tf_op jit(solution)/shard_map/ppermute | solution.py:82
  260.9 77.9 %collective-permute-start.7 = (bf16[1024,128]{1,0:T(8,128)(2,1)}, bf16[1024,128]{1,0:T(8,128)(2,1)}, u32[]{:S(2)}, u32[]{:S(2)}) collective-permute-start(bf16[1024,128]{1,0:T(8,128)(2,1)} %collective-permute-done.6), channel_id=1, source_target_pairs={{0,4},{4,8},{8,12},{12,16},{16,20},{20,24},{24,28},{28,32},{32,36}... | collective-permute-start | bytes 786440 | tf_op jit(solution)/shard_map/ppermute | solution.py:82
  299.4 77.6 %reduce-scatter.7.cloned.1.call-start = ((), (), s32[]{:S(2)}) async-start(), calls=%async_computation.7 | async-start | bytes 2621440 | tf_op jit(solution)/shard_map/reduce_scatter | solution.py:90
  338.7 70.5 %reduce-scatter.5.cloned.1.call-start = ((), (), s32[]{:S(2)}) async-start(), calls=%async_computation.6 | async-start | bytes 2621440 | tf_op jit(solution)/shard_map/reduce_scatter | solution.py:90
  (84 other events, 1733.9 us)
Sparse Core Ops, SparseCore 0:
  9.2 64.9 all-gather.1
  255.7 32.0 reduce-scatter.10
  299.5 32.0 reduce-scatter.8
  338.8 32.0 reduce-scatter.6
  377.0 32.0 reduce-scatter.4
